TPU v7x, 32 devices: a whole 2x2x4 slice. The times are simulated.
32 devices in a mesh: groups: 2 (over x), state: 16 (over z, y, core).
Axes of the slice: x: 2, y: 2, z: 4, core: 2. Of those that a mesh axis runs over, the one named last changes fastest.
Arguments:
- forward_probs: float32 [256, 8, 8192], P('groups', None, 'state'), parts along dimension 0, may hold values from 0.1 to 10
- token_ids: int32 [256, 8], P('groups'), parts along dimension 0, may hold values from 0 to 16383
- transition: bfloat16 [8192, 8192], P('state'), may hold values from 0.1 to 10
- emission: bfloat16 [8192, 16384], P('state'), may hold values from 0.05 to 20
Outputs:
- backward_probs: float32 [256, 8, 8192], P('groups', None, 'state'), parts along dimension 0
- trans_counts: float32 [16384, 8192], P(('groups', 'state')), parts along dimension 0
There are 2 independent parts, one for each index of `groups`. A program takes and returns all parts, laid end to end along the dimension named above; an argument that names none is the same for every part. Nothing has to cross between parts.
All inputs are finite; a program needn't handle non-finite values.
Results may differ from a plain program's by a relative error of at most 0.00031.
Values may be sent and summed in bfloat16 or wider, within the bound.
No kernel may reach another device: no remote copies, remote signals or barrier semaphores. Data moves between devices by JAX's collectives and lax.ppermute only.
A program may use at most 192 MiB of HBM per device.

v0:
```python
import jax
import jax.numpy as jnp
from jax import lax
from jax.sharding import PartitionSpec as P


def on_device(forward_probs, token_ids, transition, emission):
    state_rows = transition.shape[0]
    states = transition.shape[1]
    seq_count = token_ids.shape[0]
    step_count = token_ids.shape[1]
    emitted = jnp.take(emission, token_ids.reshape(-1), axis=1).astype(jnp.float32)
    emitted = emitted.reshape(state_rows, seq_count, step_count)
    backward = jnp.ones((seq_count, state_rows), jnp.float32)
    weighted = (emitted[:, :, step_count - 1].T * backward).astype(jnp.bfloat16)
    backs = [backward]
    stored = []
    scales = []
    for t in range(step_count - 2, -1, -1):
        whole = lax.all_gather(weighted, "state", axis=1, tiled=True)
        scale_sum = lax.psum(jnp.sum(weighted.astype(jnp.float32), axis=1), "state")
        product = lax.dot_general(
            whole, transition, (((1,), (1,)), ((), ())), preferred_element_type=jnp.float32
        )
        backward = product / scale_sum[:, None]
        stored.append(whole)
        scales.append(scale_sum)
        backs.append(backward)
        if t > 0:
            weighted = (emitted[:, :, t].T * backward).astype(jnp.bfloat16)
    backs = backs[::-1]
    stored = stored[::-1]
    scales = scales[::-1]
    backward_probs = jnp.stack(backs, axis=1)
    partial_norms = jnp.sum(
        forward_probs[:, : step_count - 1, :] * backward_probs[:, : step_count - 1, :], axis=2
    )
    norm_sums = lax.psum(partial_norms, "state")
    shares = []
    for t in range(step_count - 1):
        shares.append(
            (forward_probs[:, t, :] / (scales[t] * norm_sums[:, t])[:, None]).astype(jnp.bfloat16)
        )
    share_mat = jnp.concatenate(shares, axis=0)
    vector_mat = jnp.concatenate(stored, axis=0)
    moments = lax.dot_general(
        share_mat, vector_mat, (((0,), (0,)), ((), ())), preferred_element_type=jnp.float32
    )
    factor = float(states) * float(states) / float(seq_count * (step_count - 1))
    trans_counts = transition.astype(jnp.float32) * moments * factor
    return (backward_probs, trans_counts)


def solution(mesh):
    placed = (P("groups", None, "state"), P("groups", None), P("state", None), P("state", None))
    return jax.shard_map(
        on_device,
        mesh=mesh,
        in_specs=placed,
        out_specs=(P("groups", None, "state"), P(("groups", "state"), None)),
        check_vma=False,
    )
```

profile of v0, /device:TPU:0, one launch (start us, length us, event | category | flops | bytes accessed | tf_op | source)
XLA Modules:
  0.0 467.3 jit_solution(17282354931980316428)
XLA Ops:
  7.2 0.7 compare_and_fusion
  7.9 0.8 copy.15
  8.7 0.1 reshape.62
  8.8 22.4 %copy.16 = bf16[512,16384]{0,1:T(8,128)(2,1)} copy(bf16[512,16384]{1,0:T(8,128)(2,1)} %param.7) | data formatting | bytes 33554432 | tf_op args[3]
  31.2 11.9 %gather_fusion = bf16[1024,512]{1,0:T(8,128)(2,1)S(1)} fusion(bf16[512,16384]{0,1:T(8,128)(2,1)} %copy.16, s32[1024]{0:T(1024)S(1)} %broadcast_clamp_fusion), kind=kCustom, calls=%fused_computation | custom fusion | bytes 2101248 | tf_op jit(solution)/shard_map/jit(_take)/gather | solution.py:12
  43.2 0.8 fusion.41
  44.0 0.9 copy-done.9
  44.9 0.7 slice_bitcast_fusion.6
  45.7 1.0 convert_reduce_fusion.6
  46.7 35.4 %psum.56 = f32[128]{0:T(128)S(1)} all-reduce(f32[128]{0:T(128)S(1)} %convert_reduce_fusion.6), channel_id=1, replica_groups=mesh['groups'=2,'state'=16] {'state'}, use_global_device_ids=true, to_apply=%region_1.2 | all-reduce | flops 128 | bytes 1024 | tf_op jit(solution)/shard_map/psum | solution.py:21
  82.1 7.6 %all-gather.8.cloned.1.call-done = bf16[128,8192]{1,0:T(8,128)(2,1)} async-done(((bf16[128,512]{1,0:T(8,128)(2,1)}), bf16[128,8192]{1,0:T(8,128)(2,1)}) %all-gather.8.cloned.1.call-update) | async-done | bytes 2097168 | tf_op jit(solution)/shard_map/all_gather | solution.py:20
  89.7 7.7 %convert_reduce_fusion.5 = (f32[128]{0:T(128)S(1)}, bf16[128,512]{1,0:T(8,128)(2,1)}, f32[128,512]{1,0:T(8,128)}) fusion(f32[512,128,8]{0,1,2:T(8,128)S(1)} %get-tuple-element.18, f32[128]{0:T(128)S(1)} %psum.56, bf16[128,8192]{1,0:T(8,128)(2,1)} %all-gather.8.cloned.1.call-done, bf16[512,8192]{1,0:T(8,128)(2,1)} %param.6), kind=kOutput, calls=%fused_computation.69 | convolution fusion | flops 1074069376 | bytes 11142144 | tf_op jit(solution)/shard_map/dot_general | solution.py:22
  97.4 0.0 all-gather.12.cloned.1.call-start
  97.4 32.3 %psum.57 = f32[128]{0:T(128)S(1)} all-reduce(f32[128]{0:T(128)S(1)} %get-tuple-element.16), channel_id=1, replica_groups=mesh['groups'=2,'state'=16] {'state'}, use_global_device_ids=true, to_apply=%region_3.4 | all-reduce | flops 128 | bytes 1024 | tf_op jit(solution)/shard_map/psum | solution.py:21
  129.7 8.1 %all-gather.10.cloned.1.call-done = bf16[128,8192]{1,0:T(8,128)(2,1)} async-done(((bf16[128,512]{1,0:T(8,128)(2,1)}), bf16[128,8192]{1,0:T(8,128)(2,1)}) %all-gather.10.cloned.1.call-update) | async-done | bytes 2097168 | tf_op jit(solution)/shard_map/all_gather | solution.py:20
  137.8 7.7 %convert_reduce_fusion.4 = (f32[128]{0:T(128)S(1)}, bf16[128,512]{1,0:T(8,128)(2,1)}, f32[128,512]{1,0:T(8,128)}) fusion(f32[512,128,8]{0,1,2:T(8,128)S(1)} %get-tuple-element.18, f32[128]{0:T(128)S(1)} %psum.57, bf16[128,8192]{1,0:T(8,128)(2,1)} %all-gather.10.cloned.1.call-done, bf16[512,8192]{1,0:T(8,128)(2,1)} %param.6), kind=kOutput, calls=%fused_computation.68 | convolution fusion | flops 1074069376 | bytes 11142144 | tf_op jit(solution)/shard_map/dot_general | solution.py:22
  145.6 31.7 %psum.58 = f32[128]{0:T(128)S(1)} all-reduce(f32[128]{0:T(128)S(1)} %get-tuple-element.14), channel_id=1, replica_groups=mesh['groups'=2,'state'=16] {'state'}, use_global_device_ids=true, to_apply=%region_5.6 | all-reduce | flops 128 | bytes 1024 | tf_op jit(solution)/shard_map/psum | solution.py:21
  177.3 8.5 %all-gather.12.cloned.1.call-done = bf16[128,8192]{1,0:T(8,128)(2,1)} async-done(((bf16[128,512]{1,0:T(8,128)(2,1)}), bf16[128,8192]{1,0:T(8,128)(2,1)}) %all-gather.12.cloned.1.call-update) | async-done | bytes 2097168 | tf_op jit(solution)/shard_map/all_gather | solution.py:20
  185.9 7.7 %convert_reduce_fusion.3 = (f32[128]{0:T(128)S(1)}, bf16[128,512]{1,0:T(8,128)(2,1)}, f32[128,512]{1,0:T(8,128)}) fusion(f32[512,128,8]{0,1,2:T(8,128)S(1)} %get-tuple-element.18, f32[128]{0:T(128)S(1)} %psum.58, bf16[128,8192]{1,0:T(8,128)(2,1)} %all-gather.12.cloned.1.call-done, bf16[512,8192]{1,0:T(8,128)(2,1)} %param.6), kind=kOutput, calls=%fused_computation.67 | convolution fusion | flops 1074069376 | bytes 11142144 | tf_op jit(solution)/shard_map/dot_general | solution.py:22
  193.6 32.3 %psum.59 = f32[128]{0:T(128)S(1)} all-reduce(f32[128]{0:T(128)S(1)} %get-tuple-element.12), channel_id=1, replica_groups=mesh['groups'=2,'state'=16] {'state'}, use_global_device_ids=true, to_apply=%region_7.8 | all-reduce | flops 128 | bytes 1024 | tf_op jit(solution)/shard_map/psum | solution.py:21
  226.0 8.0 %all-gather.14.cloned.1.call-done = bf16[128,8192]{1,0:T(8,128)(2,1)} async-done(((bf16[128,512]{1,0:T(8,128)(2,1)}), bf16[128,8192]{1,0:T(8,128)(2,1)}) %all-gather.14.cloned.1.call-update) | async-done | bytes 2097168 | tf_op jit(solution)/shard_map/all_gather | solution.py:20
  233.9 7.7 %convert_reduce_fusion.2 = (f32[128]{0:T(128)S(1)}, bf16[128,512]{1,0:T(8,128)(2,1)}, f32[128,512]{1,0:T(8,128)}) fusion(f32[512,128,8]{0,1,2:T(8,128)S(1)} %get-tuple-element.18, f32[128]{0:T(128)S(1)} %psum.59, bf16[128,8192]{1,0:T(8,128)(2,1)} %all-gather.14.cloned.1.call-done, bf16[512,8192]{1,0:T(8,128)(2,1)} %param.6), kind=kOutput, calls=%fused_computation.66 | convolution fusion | flops 1074069376 | bytes 11142144 | tf_op jit(solution)/shard_map/dot_general | solution.py:22
  241.7 32.2 %psum.60 = f32[128]{0:T(128)S(1)} all-reduce(f32[128]{0:T(128)S(1)} %get-tuple-element.10), channel_id=1, replica_groups=mesh['groups'=2,'state'=16] {'state'}, use_global_device_ids=true, to_apply=%region_9.10 | all-reduce | flops 128 | bytes 1024 | tf_op jit(solution)/shard_map/psum | solution.py:21
  273.9 8.1 %all-gather.16.cloned.1.call-done = bf16[128,8192]{1,0:T(8,128)(2,1)} async-done(((bf16[128,512]{1,0:T(8,128)(2,1)}), bf16[128,8192]{1,0:T(8,128)(2,1)}) %all-gather.16.cloned.1.call-update) | async-done | bytes 2097168 | tf_op jit(solution)/shard_map/all_gather | solution.py:20
  282.0 7.7 %convert_reduce_fusion.1 = (f32[128]{0:T(128)S(1)}, bf16[128,512]{1,0:T(8,128)(2,1)}, f32[128,512]{1,0:T(8,128)}) fusion(f32[512,128,8]{0,1,2:T(8,128)S(1)} %get-tuple-element.18, f32[128]{0:T(128)S(1)} %psum.60, bf16[128,8192]{1,0:T(8,128)(2,1)} %all-gather.16.cloned.1.call-done, bf16[512,8192]{1,0:T(8,128)(2,1)} %param.6), kind=kOutput, calls=%fused_computation.65 | convolution fusion | flops 1074069376 | bytes 11142144 | tf_op jit(solution)/shard_map/dot_general | solution.py:22
  289.7 0.0 all-gather.20.cloned.1.call-start
  289.8 32.1 %psum.61 = f32[128]{0:T(128)S(1)} all-reduce(f32[128]{0:T(128)S(1)} %get-tuple-element.8), channel_id=1, replica_groups=mesh['groups'=2,'state'=16] {'state'}, use_global_device_ids=true, to_apply=%region_11.12 | all-reduce | flops 128 | bytes 1024 | tf_op jit(solution)/shard_map/psum | solution.py:21
  321.9 8.1 %all-gather.18.cloned.1.call-done = bf16[128,8192]{1,0:T(8,128)(2,1)} async-done(((bf16[128,512]{1,0:T(8,128)(2,1)}), bf16[128,8192]{1,0:T(8,128)(2,1)}) %all-gather.18.cloned.1.call-update) | async-done | bytes 2097168 | tf_op jit(solution)/shard_map/all_gather | solution.py:20
  330.0 7.6 %convert_reduce_fusion = (f32[128]{0:T(128)S(1)}, bf16[128,512]{1,0:T(8,128)(2,1)}, f32[128,512]{1,0:T(8,128)}) fusion(f32[512,128,8]{0,1,2:T(8,128)} %copy-done.8, f32[128]{0:T(128)S(1)} %psum.61, bf16[128,8192]{1,0:T(8,128)(2,1)} %all-gather.18.cloned.1.call-done, bf16[512,8192]{1,0:T(8,128)(2,1)} %param.6), kind=kOutput, calls=%fused_computation.64 | convolution fusion | flops 1074069376 | bytes 11142144 | tf_op jit(solution)/shard_map/dot_general | solution.py:22
  337.7 1.9 fusion.42
  339.7 32.0 %psum.62 = f32[128]{0:T(128)S(1)} all-reduce(f32[128]{0:T(128)S(1)} %get-tuple-element.6), channel_id=1, replica_groups=mesh['groups'=2,'state'=16] {'state'}, use_global_device_ids=true, to_apply=%region_13.14 | all-reduce | flops 128 | bytes 1024 | tf_op jit(solution)/shard_map/psum | solution.py:21
  371.7 6.4 %all-gather.20.cloned.1.call-done = bf16[128,8192]{1,0:T(8,128)(2,1)} async-done(((bf16[128,512]{1,0:T(8,128)(2,1)}), bf16[128,8192]{1,0:T(8,128)(2,1)}) %all-gather.20.cloned.1.call-update) | async-done | bytes 2097168 | tf_op jit(solution)/shard_map/all_gather | solution.py:20
  378.1 7.7 %constant_dynamic-update-slice_fusion.1 = (f32[128,7,512]{2,0,1:T(8,128)S(1)}, f32[128,8,512]{2,0,1:T(8,128)}) fusion(f32[128]{0:T(128)S(1)} %psum.62, bf16[128,8192]{1,0:T(8,128)(2,1)} %all-gather.20.cloned.1.call-done, bf16[512,8192]{1,0:T(8,128)(2,1)} %param.6), kind=kOutput, calls=%fused_computation.81 | convolution fusion | flops 1073807360 | bytes 11010560 | tf_op jit(solution)/shard_map/dot_general | solution.py:22
  385.9 0.7 bitcast_dynamic-update-slice_fusion.10
  386.6 0.7 bitcast_dynamic-update-slice_fusion.8
  387.4 0.7 bitcast_dynamic-update-slice_fusion.6
  388.1 0.7 bitcast_dynamic-update-slice_fusion.4
  388.9 0.7 bitcast_dynamic-update-slice_fusion.2
  389.6 0.7 bitcast_dynamic-update-slice_fusion
  390.4 1.2 fusion
  391.5 31.5 %psum.63 = f32[128,7]{0,1:T(8,128)S(1)} all-reduce(f32[128,7]{0,1:T(8,128)S(1)} %fusion), channel_id=1, replica_groups=mesh['groups'=2,'state'=16] {'state'}, use_global_device_ids=true, to_apply=%region_15.16 | all-reduce | flops 896 | bytes 7168 | tf_op jit(solution)/shard_map/psum | solution.py:38
  423.1 0.7 broadcast_dynamic-update-slice_fusion
  423.8 4.2 copy.26
  428.0 0.1 fusion.28
  428.1 0.1 fusion.29
  428.2 0.1 fusion.30
  428.3 0.1 fusion.31
  428.4 0.1 fusion.32
  428.5 0.1 fusion.33
  428.6 0.1 fusion.34
  428.7 0.9 copy-done.6
  429.6 1.5 constant_dynamic-update-slice_fusion.8
  431.1 0.9 copy-done.5
  431.9 1.5 constant_dynamic-update-slice_fusion.7
  433.4 0.9 copy-done.4
  434.3 1.5 constant_dynamic-update-slice_fusion.6
  435.8 0.9 copy-done.3
  436.6 1.5 constant_dynamic-update-slice_fusion.5
  438.1 1.5 constant_dynamic-update-slice_fusion.4
  439.6 1.3 copy-done.1
  440.9 1.5 constant_dynamic-update-slice_fusion.3
  442.4 1.5 constant_dynamic-update-slice_fusion.2
  443.9 0.8 slice-done.1
  444.6 15.9 %multiply_multiply_fusion = f32[512,8192]{1,0:T(8,128)} fusion(bf16[512,8192]{1,0:T(8,128)(2,1)S(1)} %bitcast.172, bf16[896,512]{1,0:T(8,128)(2,1)S(1)} %fusion.34, bf16[896,8192]{1,0:T(8,128)(2,1)} %constant_dynamic-update-slice_fusion.2), kind=kOutput, calls=%fused_computation.1 | convolution fusion | flops 7528775680 | bytes 40763392 | tf_op jit(solution)/shard_map/dot_general | solution.py:46
  (49 shorter events, 0.4 us)
Async XLA Ops:
  7.2 82.5 %all-gather.8.cloned.1.call-start = ((), (), s32[]{:S(2)}) async-start(), calls=%async_computation | async-start | bytes 2228224 | tf_op jit(solution)/shard_map/all_gather | solution.py:20
  43.9 1.0 copy-start.9
  43.9 238.1 %copy-start.8 = (f32[512,128,8]{0,1,2:T(8,128)}, f32[512,128,8]{0,1,2:T(8,128)S(1)}, u32[]{:S(2)}) copy-start(f32[512,128,8]{0,1,2:T(8,128)S(1)} %get-tuple-element.18) | copy-start | bytes 6291460
  45.6 92.2 %all-gather.10.cloned.1.call-start = ((), (), s32[]{:S(2)}) async-start(), calls=%async_computation.1 | async-start | bytes 2228224 | tf_op jit(solution)/shard_map/all_gather | solution.py:20
  97.4 88.5 %all-gather.12.cloned.1.call-start = ((), (), s32[]{:S(2)}) async-start(), calls=%async_computation.2 | async-start | bytes 2228224 | tf_op jit(solution)/shard_map/all_gather | solution.py:20
  145.6 88.4 %all-gather.14.cloned.1.call-start = ((), (), s32[]{:S(2)}) async-start(), calls=%async_computation.3 | async-start | bytes 2228224 | tf_op jit(solution)/shard_map/all_gather | solution.py:20
  193.6 88.4 %all-gather.16.cloned.1.call-start = ((), (), s32[]{:S(2)}) async-start(), calls=%async_computation.4 | async-start | bytes 2228224 | tf_op jit(solution)/shard_map/all_gather | solution.py:20
  241.6 88.4 %all-gather.18.cloned.1.call-start = ((), (), s32[]{:S(2)}) async-start(), calls=%async_computation.5 | async-start | bytes 2228224 | tf_op jit(solution)/shard_map/all_gather | solution.py:20
  289.7 88.4 %all-gather.20.cloned.1.call-start = ((), (), s32[]{:S(2)}) async-start(), calls=%async_computation.6 | async-start | bytes 2228224 | tf_op jit(solution)/shard_map/all_gather | solution.py:20
  321.9 15.8 %copy-start.7 = (f32[128,8,512]{2,1,0:T(8,128)S(1)}, f32[128,8,512]{2,1,0:T(8,128)}, u32[]{:S(2)}) copy-start(f32[128,8,512]{2,1,0:T(8,128)} %param.4) | copy-start | bytes 6291460
  378.1 7.7 %copy-start.17 = (f32[128,512]{1,0:T(8,128)S(1)}, f32[128,512]{1,0:T(8,128)}, u32[]{:S(2)}) copy-start(f32[128,512]{1,0:T(8,128)} %get-tuple-element.53) | copy-start | bytes 786436
  378.1 8.5 %copy-start.16 = (f32[128,512]{1,0:T(8,128)S(1)}, f32[128,512]{1,0:T(8,128)}, u32[]{:S(2)}) copy-start(f32[128,512]{1,0:T(8,128)} %get-tuple-element.52) | copy-start | bytes 786436
  378.1 9.2 %copy-start.15 = (f32[128,512]{1,0:T(8,128)S(1)}, f32[128,512]{1,0:T(8,128)}, u32[]{:S(2)}) copy-start(f32[128,512]{1,0:T(8,128)} %get-tuple-element.51) | copy-start | bytes 786436
  385.9 2.3 copy-start.14
  385.9 3.0 copy-start.13
  385.9 3.7 copy-start.12
  423.8 4.2 copy-start.11
  423.8 4.3 copy-start.10
  428.0 1.6 copy-start.6
  429.6 2.3 copy-start.5
  431.9 2.3 copy-start.4
  434.3 2.3 copy-start.3
  434.3 3.8 copy-start.2
  436.6 7.3 %slice-start = ((s8[8388608]{0:T(1024)(128)(4,1)}), s8[4194304]{0:T(1024)(128)(4,1)S(1)}, s32[]{:S(2)}) async-start(s8[8388608]{0:T(1024)(128)(4,1)} %bitcast.171), calls=%async_computation.7 | async-start | bytes 8388608
  438.1 2.8 copy-start.1
  438.1 4.3 copy-start
  440.9 3.7 slice-start.1
Sparse Core Ops, SparseCore 0:
  45.7 43.8 all-gather.7
  97.5 40.2 all-gather.9
  145.7 40.1 all-gather.11
  193.7 40.1 all-gather.13
  241.8 40.1 all-gather.15
  289.8 40.1 all-gather.17
  337.8 40.2 all-gather.19
where the time goes:
time: 468 us; the launch traced here: 467 us
  blocking collectives  260 us (56%)
  matrix products  69.7 us (15%)
  local copies, waits for them, and re-layouts  64.2 us (14%)
  waiting for transfers between devices  55 us (12%)
  between operations  14.3 us (3%)
    psum x7, blocking collectives, on_device(): scale_sum = lax.psum(jnp.sum(weighted.astype(jnp.float32), axis=1), 'state')  228 us
    all_gather x7, waiting for transfers between devices, on_device(): whole = lax.all_gather(weighted, 'state', axis=1, tiled=True)  54.9 us
    dot_general x7, matrix products, on_device(): lax.dot_general(whole, transition, (((1,), (1,)), ((), ())), preferred_el...  53.8 us
    unnamed x54, local copies, waits for them, and re-layouts  46.6 us
    psum x1, blocking collectives, on_device(): norm_sums = lax.psum(partial_norms, 'state')  31.5 us
    dot_general x1, matrix products, on_device(): lax.dot_general(share_mat, vector_mat, (((0,), (0,)), ((), ())), preferre...  15.9 us
    gather x1, local copies, waits for them, and re-layouts, on_device(): jnp.take(emission, token_ids.reshape(-1), axis=1).astype(jnp.float32)  11.9 us
  transfers between devices with their start and end apart: 7, of which 7 were waited for; matrix products, arithmetic and copies ran while one was open for 1% of the time, Pallas kernels for 0%

commit v1 on v0

--- a/solution.py
+++ b/solution.py
@@ -17,7 +17,14 @@
     stored = []
     scales = []
     for t in range(step_count - 2, -1, -1):
-        whole = lax.all_gather(weighted, "state", axis=1, tiled=True)
+        n_dev = lax.axis_size("state")
+        right = [(i, (i + 1) % n_dev) for i in range(n_dev)]
+        parts = [weighted]
+        for reach in range(1, n_dev):
+            parts = [lax.ppermute(parts[0], "state", right), *parts]
+        out = jnp.concatenate(parts, axis=1)
+        shift = (lax.axis_index("state") + 1) * parts[-1].shape[1]
+        whole = jnp.roll(out, shift, axis=1)
         scale_sum = lax.psum(jnp.sum(weighted.astype(jnp.float32), axis=1), "state")
         product = lax.dot_general(
             whole, transition, (((1,), (1,)), ((), ())), preferred_element_type=jnp.float32

time: 468 us -> 1160 us (2.48)
  waiting for transfers between devices: 55 us -> 696 us
  local copies, waits for them, and re-layouts: 64.2 us -> 88.3 us
  other arithmetic: 4.29 us -> 21.2 us
  between operations: 14.3 us -> 2.16 us
    ppermute x0 -> x105, waiting for transfers between devices: none -> 696 us  [on_device(): parts = [lax.ppermute(parts[0], 'state', right), *parts]]
    all_gather x7 -> x0, waiting for transfers between devices: 54.9 us -> none  [on_device(): whole = lax.all_gather(weighted, 'state', axis=1, tiled=True)]
    unnamed x54 -> x241, local copies, waits for them, and re-layouts: 46.6 us -> 71.9 us
    unnamed x7 -> x13, other arithmetic: 0.54 us -> 15.1 us
  transfers between devices with their start and end apart: 7 -> 105, of which waited for: 7 -> 98; matrix products, arithmetic and copies ran while one was open for 1% -> 0% of each run, Pallas kernels for 0% -> 0%
where the time goes in v1:
time: 1160 us; the launch traced here: 1150 us
  waiting for transfers between devices  696 us (60%)
  blocking collectives  269 us (23%)
  local copies, waits for them, and re-layouts  88.3 us (8%)
  matrix products  72.1 us (6%)
  other arithmetic  21.2 us (2%)
    ppermute x105, waiting for transfers between devices, on_device(): parts = [lax.ppermute(parts[0], 'state', right), *parts]  696 us
    psum x7, blocking collectives, on_device(): scale_sum = lax.psum(jnp.sum(weighted.astype(jnp.float32), axis=1), 'state')  239 us
    unnamed x241, local copies, waits for them, and re-layouts  71.9 us
    dot_general x7, matrix products, on_device(): lax.dot_general(whole, transition, (((1,), (1,)), ((), ())), preferred_el...  56 us
    psum x1, blocking collectives, on_device(): norm_sums = lax.psum(partial_norms, 'state')  29.5 us
  transfers between devices with their start and end apart: 105, of which 98 were waited for; matrix products, arithmetic and copies ran while one was open for 0% of the time, Pallas kernels for 0%

profile of v1, /device:TPU:0, one launch (start us, length us, event | category | flops | bytes accessed | tf_op | source)
XLA Modules:
  0.0 1149.6 jit_solution(10681602850477885260)
XLA Ops:
  2.2 22.4 %copy.16 = bf16[512,16384]{0,1:T(8,128)(2,1)} copy(bf16[512,16384]{1,0:T(8,128)(2,1)} %param.9) | data formatting | bytes 33554432 | tf_op args[3]
  24.7 11.9 %gather_fusion = bf16[1024,512]{1,0:T(8,128)(2,1)S(1)} fusion(bf16[512,16384]{0,1:T(8,128)(2,1)} %copy.16, s32[1024]{0:T(1024)S(1)} %broadcast_clamp_fusion), kind=kCustom, calls=%fused_computation | custom fusion | bytes 2101248 | tf_op jit(solution)/shard_map/jit(_take)/gather | solution.py:12
  38.8 7.6 collective-permute-done
  46.5 7.1 collective-permute-done.1
  53.6 7.1 collective-permute-done.2
  60.7 7.1 collective-permute-done.3
  67.8 7.1 collective-permute-done.4
  74.8 7.1 collective-permute-done.5
  81.9 7.1 collective-permute-done.6
  89.0 7.1 collective-permute-done.7
  96.1 7.1 collective-permute-done.8
  103.2 7.1 collective-permute-done.9
  110.3 7.1 collective-permute-done.10
  117.4 7.1 collective-permute-done.11
  125.1 7.1 collective-permute-done.12
  132.9 7.2 collective-permute-done.13
  141.1 33.9 %psum.56 = f32[128]{0:T(128)S(1)} all-reduce(f32[128]{0:T(128)S(1)} %convert_reduce_fusion.6), channel_id=1, replica_groups=mesh['groups'=2,'state'=16] {'state'}, use_global_device_ids=true, to_apply=%region_1.3 | all-reduce | flops 128 | bytes 1024 | tf_op jit(solution)/shard_map/psum | solution.py:28
  179.8 7.8 convert_reduce_fusion.5
  187.7 7.1 collective-permute-done.15
  194.8 7.1 collective-permute-done.16
  201.9 7.1 collective-permute-done.17
  208.9 7.1 collective-permute-done.18
  216.0 7.1 collective-permute-done.19
  223.1 7.1 collective-permute-done.20
  230.2 7.1 collective-permute-done.21
  237.3 7.1 collective-permute-done.22
  244.4 7.1 collective-permute-done.23
  251.5 7.1 collective-permute-done.24
  258.6 7.1 collective-permute-done.25
  266.3 7.1 collective-permute-done.26
  274.0 7.1 collective-permute-done.27
  281.8 7.2 collective-permute-done.28
  289.0 34.1 %psum.57 = f32[128]{0:T(128)S(1)} all-reduce(f32[128]{0:T(128)S(1)} %get-tuple-element.17), channel_id=1, replica_groups=mesh['groups'=2,'state'=16] {'state'}, use_global_device_ids=true, to_apply=%region_3.5 | all-reduce | flops 128 | bytes 1024 | tf_op jit(solution)/shard_map/psum | solution.py:28
  327.9 7.9 convert_reduce_fusion.4
  335.8 7.1 collective-permute-done.30
  342.9 7.1 collective-permute-done.31
  350.0 7.1 collective-permute-done.32
  357.1 7.1 collective-permute-done.33
  364.1 7.1 collective-permute-done.34
  371.2 7.1 collective-permute-done.35
  378.3 7.1 collective-permute-done.36
  385.4 7.1 collective-permute-done.37
  392.5 7.1 collective-permute-done.38
  429.9 7.2 collective-permute-done.43
  437.2 33.9 %psum.58 = f32[128]{0:T(128)S(1)} all-reduce(f32[128]{0:T(128)S(1)} %get-tuple-element.15), channel_id=1, replica_groups=mesh['groups'=2,'state'=16] {'state'}, use_global_device_ids=true, to_apply=%region_5.7 | all-reduce | flops 128 | bytes 1024 | tf_op jit(solution)/shard_map/psum | solution.py:28
  475.9 8.4 convert_reduce_fusion.3
  548.0 7.1 collective-permute-done.54
  578.3 7.2 collective-permute-done.58
  585.6 34.0 %psum.59 = f32[128]{0:T(128)S(1)} all-reduce(f32[128]{0:T(128)} %get-tuple-element.13), channel_id=1, replica_groups=mesh['groups'=2,'state'=16] {'state'}, use_global_device_ids=true, to_apply=%region_7.9 | all-reduce | flops 128 | bytes 1024 | tf_op jit(solution)/shard_map/psum | solution.py:28
  624.4 8.4 convert_reduce_fusion.2
  719.6 7.1 collective-permute-done.72
  727.4 7.2 collective-permute-done.73
  734.6 34.6 %psum.60 = f32[128]{0:T(128)} all-reduce(f32[128]{0:T(128)} %get-tuple-element.11), channel_id=1, replica_groups=mesh['groups'=2,'state'=16] {'state'}, use_global_device_ids=true, to_apply=%region_9.11 | all-reduce | flops 128 | bytes 1024 | tf_op jit(solution)/shard_map/psum | solution.py:28
  774.0 7.8 convert_reduce_fusion.1
  859.9 7.1 collective-permute-done.86
  874.1 7.1 collective-permute-done.88
  881.2 33.9 %psum.61 = f32[128]{0:T(128)S(1)} all-reduce(f32[128]{0:T(128)S(1)} %get-tuple-element.9), channel_id=1, replica_groups=mesh['groups'=2,'state'=16] {'state'}, use_global_device_ids=true, to_apply=%region_11.13 | all-reduce | flops 128 | bytes 1024 | tf_op jit(solution)/shard_map/psum | solution.py:28
  915.7 8.4 convert_reduce_fusion
  966.6 7.1 collective-permute-done.96
  1016.3 7.2 collective-permute-done.103
  1025.6 34.8 %psum.62 = f32[128]{0:T(128)} all-reduce(f32[128]{0:T(128)} %get-tuple-element.7), channel_id=1, replica_groups=mesh['groups'=2,'state'=16] {'state'}, use_global_device_ids=true, to_apply=%region_13.15 | all-reduce | flops 128 | bytes 1024 | tf_op jit(solution)/shard_map/psum | solution.py:28
  1070.5 7.3 constant_dynamic-update-slice_fusion.126
  1083.5 29.5 %psum.63 = f32[128,7]{0,1:T(8,128)S(1)} all-reduce(f32[128,7]{0,1:T(8,128)S(1)} %fusion.7), channel_id=1, replica_groups=mesh['groups'=2,'state'=16] {'state'}, use_global_device_ids=true, to_apply=%region_15.17 | all-reduce | flops 896 | bytes 7168 | tf_op jit(solution)/shard_map/psum | solution.py:45
  1133.2 16.1 %multiply_multiply_fusion = f32[512,8192]{1,0:T(8,128)} fusion(bf16[512,8192]{1,0:T(8,128)(2,1)S(1)} %bitcast.167, bf16[896,512]{1,0:T(8,128)(2,1)S(1)} %constant_dynamic-update-slice_fusion.127, bf16[896,8192]{1,0:T(8,128)(2,1)} %constant_dynamic-update-slice_fusion.134), kind=kOutput, calls=%fused_computation.1 | convolution fusion | flops 7528775680 | bytes 40763392 | tf_op jit(solution)/shard_map/dot_general | solution.py:53
  (438 shorter events, 444.9 us)
Async XLA Ops:
  38.3 8.2 collective-permute-start
  46.5 7.1 collective-permute-start.1
  53.6 7.1 collective-permute-start.2
  60.7 7.1 collective-permute-start.3
  67.8 7.1 collective-permute-start.4
  74.8 7.1 collective-permute-start.5
  81.9 7.1 collective-permute-start.6
  89.0 7.1 collective-permute-start.7
  96.1 7.1 collective-permute-start.8
  103.2 7.1 collective-permute-start.9
  110.3 7.1 collective-permute-start.10
  117.4 7.1 collective-permute-start.11
  125.1 7.1 collective-permute-start.12
  132.9 7.2 collective-permute-start.13
  140.1 34.9 %collective-permute-start.14 = (bf16[128,512]{1,0:T(8,128)(2,1)}, bf16[128,512]{1,0:T(8,128)(2,1)}, u32[]{:S(2)}, u32[]{:S(2)}) collective-permute-start(bf16[128,512]{1,0:T(8,128)(2,1)} %collective-permute-done.13), channel_id=1, source_target_pairs={{0,1},{1,2},{2,3},{3,4},{4,5},{5,6},{6,7},{7,8},{8,9},{9,10},{10,1... | collective-permute-start | bytes 393224 | tf_op jit(solution)/shard_map/ppermute | solution.py:24
  187.7 7.1 collective-permute-start.15
  194.8 7.1 collective-permute-start.16
  201.8 7.1 collective-permute-start.17
  208.9 7.1 collective-permute-start.18
  216.0 7.1 collective-permute-start.19
  223.1 7.1 collective-permute-start.20
  230.2 7.1 collective-permute-start.21
  237.3 7.1 collective-permute-start.22
  244.4 7.1 collective-permute-start.23
  251.5 7.1 collective-permute-start.24
  258.6 7.1 collective-permute-start.25
  266.3 7.1 collective-permute-start.26
  274.0 7.1 collective-permute-start.27
  281.8 7.2 collective-permute-start.28
  289.0 34.1 %collective-permute-start.29 = (bf16[128,512]{1,0:T(8,128)(2,1)}, bf16[128,512]{1,0:T(8,128)(2,1)}, u32[]{:S(2)}, u32[]{:S(2)}) collective-permute-start(bf16[128,512]{1,0:T(8,128)(2,1)} %collective-permute-done.28), channel_id=1, source_target_pairs={{0,1},{1,2},{2,3},{3,4},{4,5},{5,6},{6,7},{7,8},{8,9},{9,10},{10,1... | collective-permute-start | bytes 393224 | tf_op jit(solution)/shard_map/ppermute | solution.py:24
  335.8 7.1 collective-permute-start.30
  342.9 7.1 collective-permute-start.31
  350.0 7.1 collective-permute-start.32
  357.0 7.1 collective-permute-start.33
  364.1 7.1 collective-permute-start.34
  371.2 7.1 collective-permute-start.35
  378.3 7.1 collective-permute-start.36
  385.4 7.1 collective-permute-start.37
  392.5 7.1 collective-permute-start.38
  399.6 7.1 collective-permute-start.39
  406.7 7.1 collective-permute-start.40
  414.4 7.1 collective-permute-start.41
  422.2 7.1 collective-permute-start.42
  429.9 7.2 collective-permute-start.43
  437.1 33.9 %collective-permute-start.44 = (bf16[128,512]{1,0:T(8,128)(2,1)}, bf16[128,512]{1,0:T(8,128)(2,1)}, u32[]{:S(2)}, u32[]{:S(2)}) collective-permute-start(bf16[128,512]{1,0:T(8,128)(2,1)} %collective-permute-done.43), channel_id=1, source_target_pairs={{0,1},{1,2},{2,3},{3,4},{4,5},{5,6},{6,7},{7,8},{8,9},{9,10},{10,1... | collective-permute-start | bytes 393224 | tf_op jit(solution)/shard_map/ppermute | solution.py:24
  484.2 7.1 collective-permute-start.45
  491.3 7.1 collective-permute-start.46
  498.4 7.1 collective-permute-start.47
  505.5 7.1 collective-permute-start.48
  512.6 7.1 collective-permute-start.49
  519.7 7.1 collective-permute-start.50
  526.8 7.1 collective-permute-start.51
  533.8 7.1 collective-permute-start.52
  540.9 7.1 collective-permute-start.53
  548.0 7.1 collective-permute-start.54
  578.3 7.2 collective-permute-start.58
  585.6 34.0 %collective-permute-start.59 = (bf16[128,512]{1,0:T(8,128)(2,1)}, bf16[128,512]{1,0:T(8,128)(2,1)}, u32[]{:S(2)}, u32[]{:S(2)}) collective-permute-start(bf16[128,512]{1,0:T(8,128)(2,1)} %collective-permute-done.58), channel_id=1, source_target_pairs={{0,1},{1,2},{2,3},{3,4},{4,5},{5,6},{6,7},{7,8},{8,9},{9,10},{10,1... | collective-permute-start | bytes 393224 | tf_op jit(solution)/shard_map/ppermute | solution.py:24
  711.5 7.5 collective-permute-start.71
  727.4 7.2 collective-permute-start.73
  734.6 34.6 %collective-permute-start.74 = (bf16[128,512]{1,0:T(8,128)(2,1)}, bf16[128,512]{1,0:T(8,128)(2,1)}, u32[]{:S(2)}, u32[]{:S(2)}) collective-permute-start(bf16[128,512]{1,0:T(8,128)(2,1)} %collective-permute-done.73), channel_id=1, source_target_pairs={{0,1},{1,2},{2,3},{3,4},{4,5},{5,6},{6,7},{7,8},{8,9},{9,10},{10,1... | collective-permute-start | bytes 393224 | tf_op jit(solution)/shard_map/ppermute | solution.py:24
  874.1 7.1 collective-permute-start.88
  881.2 33.9 %collective-permute-start.89 = (bf16[128,512]{1,0:T(8,128)(2,1)S(1)}, bf16[128,512]{1,0:T(8,128)(2,1)S(1)}, u32[]{:S(2)}, u32[]{:S(2)}) collective-permute-start(bf16[128,512]{1,0:T(8,128)(2,1)S(1)} %collective-permute-done.88), channel_id=1, source_target_pairs={{0,1},{1,2},{2,3},{3,4},{4,5},{5,6},{6,7},{7,8},{8,9},{9,10},{10,1... | collective-permute-start | bytes 393224 | tf_op jit(solution)/shard_map/ppermute | solution.py:24
  1016.3 7.2 collective-permute-start.103
  1023.6 36.8 %collective-permute-start.104 = (bf16[128,512]{1,0:T(8,128)(2,1)}, bf16[128,512]{1,0:T(8,128)(2,1)}, u32[]{:S(2)}, u32[]{:S(2)}) collective-permute-start(bf16[128,512]{1,0:T(8,128)(2,1)} %collective-permute-done.103), channel_id=1, source_target_pairs={{0,1},{1,2},{2,3},{3,4},{4,5},{5,6},{6,7},{7,8},{8,9},{9,10},{10,1... | collective-permute-start | bytes 393224 | tf_op jit(solution)/shard_map/ppermute | solution.py:24
  (105 other events, 2036.4 us)
